TPU v7x, 32 devices: a whole 2x2x4 slice. The times are simulated.
32 devices in a mesh: row: 4 (over z), col: 8 (over y, x, core).
Axes of the slice: x: 2, y: 2, z: 4, core: 2. Of those that a mesh axis runs over, the one named last changes fastest.
Arguments:
- layer_input: bfloat16 [8192, 2048], P(('col', 'row')), may hold values from -6 to 6
- w_query: bfloat16 [2048, 2048], P('col', 'row'), may hold values from -0.125 to 0.125
- w_key: bfloat16 [2048, 2048], P('col', 'row'), may hold values from -0.125 to 0.125
- w_value: bfloat16 [2048, 2048], P('col', 'row'), may hold values from -0.125 to 0.125
- w_output: bfloat16 [2048, 2048], P('row', 'col'), may hold values from -1.5 to 1.5
- w_gate: bfloat16 [2048, 8192], P('col', 'row'), may hold values from -0.125 to 0.125
- w_up: bfloat16 [2048, 8192], P('col', 'row'), may hold values from -0.125 to 0.125
- w_down: bfloat16 [8192, 2048], P('row', 'col'), may hold values from -0.0625 to 0.0625
- piece_starts: int32 [8, 2], P('col'), may hold values from 0 to 768, as said below
- cotangent: bfloat16 [8192, 2048], P(('col', 'row')), may hold values from -6 to 6
Outputs:
- output: bfloat16 [8192, 2048], P(('col', 'row'))
- input_grad: float32 [8192, 2048], P(('col', 'row'))
- grad_w_query: float32 [2048, 2048], P('col', 'row')
- grad_w_key: float32 [2048, 2048], P('col', 'row')
- grad_w_value: float32 [2048, 2048], P('col', 'row')
- grad_w_output: float32 [2048, 2048], P('row', 'col')
- grad_w_gate: float32 [2048, 8192], P('col', 'row')
- grad_w_up: float32 [2048, 8192], P('col', 'row')
- grad_w_down: float32 [8192, 2048], P('row', 'col')
Inputs may be any that keep to these rules, and one draw needn't show every extreme that they name: `piece_starts`: piece p of a sequence starts at p * 512 or later and ends by (p + 1) * 512, so the pieces of one sequence do not intersect.
All inputs are finite; a program needn't handle non-finite values.
Results may differ from a plain program's by a relative error of at most 0.019.
Values may be sent and summed in bfloat16 or wider, within the bound.
No kernel may reach another device: no remote copies, remote signals or barrier semaphores. Data moves between devices by JAX's collectives and lax.ppermute only.
A program may use at most 256 MiB of HBM per device.

v0:
```python
import math
import jax
import jax.numpy as jnp
from jax import lax
from jax.sharding import PartitionSpec as P

HD = 128
LENGTH = 1024
PIECE = 256
EPSILON = 1e-05
NEGATIVE = -1e30


def product(left, right):
    return jnp.dot(left, right, preferred_element_type=jnp.float32)


def contract_rows(left, right):
    return lax.dot_general(
        left, right, (((0,), (0,)), ((), ())), preferred_element_type=jnp.float32
    )


def times_transpose(left, right):
    return lax.dot_general(
        left, right, (((1,), (1,)), ((), ())), preferred_element_type=jnp.float32
    )


def layer_norm(inputs):
    center = inputs - jnp.mean(inputs, axis=-1, keepdims=True)
    spread = jnp.mean(center * center, axis=-1, keepdims=True)
    return center * lax.rsqrt(spread + EPSILON)


def norm_back(inputs, grad):
    center = inputs - jnp.mean(inputs, axis=-1, keepdims=True)
    inverse = lax.rsqrt(jnp.mean(center * center, axis=-1, keepdims=True) + EPSILON)
    normed = center * inverse
    return inverse * (
        grad
        - jnp.mean(grad, axis=-1, keepdims=True)
        - normed * jnp.mean(grad * normed, axis=-1, keepdims=True)
    )


def rope_tables():
    positions = jnp.arange(LENGTH, dtype=jnp.float32)
    freqs = jnp.power(jnp.float32(10000.0), -jnp.arange(HD // 2, dtype=jnp.float32) * (2.0 / HD))
    angles = positions[:, None] * freqs[None, :]
    return (jnp.cos(angles)[:, None, :], jnp.sin(angles)[:, None, :])


def rotate(field, cosine, sine):
    half_size = field.shape[-1] // 2
    first_half = field[..., :half_size]
    second_half = field[..., half_size:]
    return jnp.concatenate(
        [first_half * cosine - second_half * sine, second_half * cosine + first_half * sine],
        axis=-1,
    )


def unrotate(field, cosine, sine):
    half_size = field.shape[-1] // 2
    first_half = field[..., :half_size]
    second_half = field[..., half_size:]
    return jnp.concatenate(
        [first_half * cosine + second_half * sine, second_half * cosine - first_half * sine],
        axis=-1,
    )


def piece_mask(starts):
    positions = jnp.arange(LENGTH, dtype=jnp.int32)
    inside = (positions[None, :] >= starts[:, None]) & (
        positions[None, :] < starts[:, None] + PIECE
    )
    shared = jnp.any(inside[:, :, None] & inside[:, None, :], axis=0)
    causal = positions[None, :] <= positions[:, None]
    return causal | shared


def masked_scores(queries, keys_rot, starts):
    scale = 1.0 / math.sqrt(HD)
    scores = (
        jnp.einsum("qhd,khd->hqk", queries, keys_rot, preferred_element_type=jnp.float32) * scale
    )
    return jnp.where(piece_mask(starts)[None], scores, NEGATIVE)


def attend_forward(operands):
    queries, keys_rot, values, starts = operands
    scores = masked_scores(queries, keys_rot, starts)
    row_top = jnp.max(scores, axis=-1, keepdims=True)
    shifted = jnp.exp(scores - row_top)
    row_total = jnp.sum(shifted, axis=-1, keepdims=True)
    probs = (shifted / row_total).astype(jnp.bfloat16)
    mixed = jnp.einsum("hqk,khd->qhd", probs, values, preferred_element_type=jnp.float32)
    return (mixed, row_top + jnp.log(row_total))


def attend_backward(operands):
    queries, keys_rot, values, starts, log_total, grad_mixed = operands
    scale = 1.0 / math.sqrt(HD)
    scores = masked_scores(queries, keys_rot, starts)
    probs = jnp.exp(scores - log_total)
    probs_low = probs.astype(jnp.bfloat16)
    grad_values = jnp.einsum(
        "hqk,qhd->khd", probs_low, grad_mixed, preferred_element_type=jnp.float32
    )
    grad_probs = jnp.einsum("qhd,khd->hqk", grad_mixed, values, preferred_element_type=jnp.float32)
    inner = jnp.sum(probs * grad_probs, axis=-1, keepdims=True)
    grad_scores = (probs * (grad_probs - inner)).astype(jnp.bfloat16)
    grad_queries = (
        jnp.einsum("hqk,khd->qhd", grad_scores, keys_rot, preferred_element_type=jnp.float32)
        * scale
    )
    grad_keys = (
        jnp.einsum("hqk,qhd->khd", grad_scores, queries, preferred_element_type=jnp.float32) * scale
    )
    return (grad_queries, grad_keys, grad_values)


def per_device(
    layer_input, w_query, w_key, w_value, w_output, w_gate, w_up, w_down, piece_starts, cotangent
):
    seq_count = piece_starts.shape[0]
    group_rows = seq_count * LENGTH
    heads_local = w_query.shape[1] // HD
    gathered = (
        lax.all_gather(w_query, "col", axis=0, tiled=True),
        lax.all_gather(w_key, "col", axis=0, tiled=True),
        lax.all_gather(w_value, "col", axis=0, tiled=True),
        lax.all_gather(w_output, "col", axis=1, tiled=True),
        lax.all_gather(w_gate, "col", axis=0, tiled=True),
        lax.all_gather(w_up, "col", axis=0, tiled=True),
        lax.all_gather(w_down, "col", axis=1, tiled=True),
    )
    full_query, full_key, full_value, full_output, full_gate, full_up, full_down = gathered
    cosine, sine = rope_tables()
    inputs = layer_input.astype(jnp.float32)
    normed_first = layer_norm(inputs).astype(jnp.bfloat16)
    first_rows = lax.all_gather(normed_first, "row", axis=0, tiled=True)

    def split_heads(matrix):
        return matrix.reshape(seq_count, LENGTH, heads_local, HD)

    def merge_heads(field):
        return field.reshape(group_rows, heads_local * HD)

    queries = rotate(split_heads(product(first_rows, full_query)), cosine, sine).astype(
        jnp.bfloat16
    )
    keys_rot = rotate(split_heads(product(first_rows, full_key)), cosine, sine).astype(jnp.bfloat16)
    values = split_heads(product(first_rows, full_value)).astype(jnp.bfloat16)
    mixed, log_total = lax.map(attend_forward, (queries, keys_rot, values, piece_starts))
    attended = merge_heads(mixed.astype(jnp.bfloat16))
    attention_sum = lax.psum_scatter(
        product(attended, full_output), "row", scatter_dimension=0, tiled=True
    )
    middle = inputs + attention_sum
    normed_second = layer_norm(middle).astype(jnp.bfloat16)
    second_rows = lax.all_gather(normed_second, "row", axis=0, tiled=True)
    gate_lin = product(second_rows, full_gate)
    up_lin = product(second_rows, full_up)
    activation = (jax.nn.silu(gate_lin) * up_lin).astype(jnp.bfloat16)
    ffn_sum = lax.psum_scatter(
        product(activation, full_down).astype(jnp.bfloat16), "row", scatter_dimension=0, tiled=True
    ).astype(jnp.float32)
    output = (middle + ffn_sum).astype(jnp.bfloat16)
    back_query, back_key, back_value, back_output = (full_query, full_key, full_value, full_output)
    back_gate, back_up, back_down = (full_gate, full_up, full_down)
    grad_rows = lax.all_gather(cotangent, "row", axis=0, tiled=True)
    grad_activation = times_transpose(grad_rows, back_down)
    sigma = jax.nn.sigmoid(gate_lin)
    grad_gate = (grad_activation * up_lin * sigma * (1.0 + gate_lin * (1.0 - sigma))).astype(
        jnp.bfloat16
    )
    grad_up = (grad_activation * gate_lin * sigma).astype(jnp.bfloat16)
    grad_second = lax.psum_scatter(
        (times_transpose(grad_gate, back_gate) + times_transpose(grad_up, back_up)).astype(
            jnp.bfloat16
        ),
        "row",
        scatter_dimension=0,
        tiled=True,
    ).astype(jnp.float32)
    grad_middle = cotangent.astype(jnp.float32) + norm_back(middle, grad_second)
    grad_branch = lax.all_gather(grad_middle.astype(jnp.bfloat16), "row", axis=0, tiled=True)
    grad_mixed = split_heads(times_transpose(grad_branch, back_output).astype(jnp.bfloat16))
    grad_q_rot, grad_k_rot, grad_values = lax.map(
        attend_backward, (queries, keys_rot, values, piece_starts, log_total, grad_mixed)
    )
    grad_query = merge_heads(unrotate(grad_q_rot, cosine, sine)).astype(jnp.bfloat16)
    grad_key = merge_heads(unrotate(grad_k_rot, cosine, sine)).astype(jnp.bfloat16)
    grad_value = merge_heads(grad_values).astype(jnp.bfloat16)
    grad_first = lax.psum_scatter(
        (
            times_transpose(grad_query, back_query)
            + times_transpose(grad_key, back_key)
            + times_transpose(grad_value, back_value)
        ).astype(jnp.bfloat16),
        "row",
        scatter_dimension=0,
        tiled=True,
    ).astype(jnp.float32)
    grad_input = grad_middle + norm_back(inputs, grad_first)
    grad_query_w = contract_rows(first_rows, grad_query)
    grad_key_w = contract_rows(first_rows, grad_key)
    grad_value_w = contract_rows(first_rows, grad_value)
    grad_output_w = contract_rows(attended, grad_branch)
    grad_gate_w = contract_rows(second_rows, grad_gate)
    grad_up_w = contract_rows(second_rows, grad_up)
    grad_down_w = contract_rows(activation, grad_rows)
    summed = (
        lax.psum_scatter(
            grad_query_w.astype(jnp.bfloat16), "col", scatter_dimension=0, tiled=True
        ).astype(jnp.float32),
        lax.psum_scatter(
            grad_key_w.astype(jnp.bfloat16), "col", scatter_dimension=0, tiled=True
        ).astype(jnp.float32),
        lax.psum_scatter(
            grad_value_w.astype(jnp.bfloat16), "col", scatter_dimension=0, tiled=True
        ).astype(jnp.float32),
        lax.psum_scatter(
            grad_output_w.astype(jnp.bfloat16), "col", scatter_dimension=1, tiled=True
        ).astype(jnp.float32),
        lax.psum_scatter(
            grad_gate_w.astype(jnp.bfloat16), "col", scatter_dimension=0, tiled=True
        ).astype(jnp.float32),
        lax.psum_scatter(
            grad_up_w.astype(jnp.bfloat16), "col", scatter_dimension=0, tiled=True
        ).astype(jnp.float32),
        lax.psum_scatter(
            grad_down_w.astype(jnp.bfloat16), "col", scatter_dimension=1, tiled=True
        ).astype(jnp.float32),
    )
    results = tuple(summed)
    return (
        output,
        grad_input,
        results[0],
        results[1],
        results[2],
        results[3],
        results[4],
        results[5],
        results[6],
    )


def solution(mesh):
    in_specs = (
        P(("col", "row"), None),
        P("col", "row"),
        P("col", "row"),
        P("col", "row"),
        P("row", "col"),
        P("col", "row"),
        P("col", "row"),
        P("row", "col"),
        P("col", None),
        P(("col", "row"), None),
    )
    out_specs = (
        P(("col", "row"), None),
        P(("col", "row"), None),
        P("col", "row"),
        P("col", "row"),
        P("col", "row"),
        P("row", "col"),
        P("col", "row"),
        P("col", "row"),
        P("row", "col"),
    )
    return jax.shard_map(
        per_device, mesh=mesh, in_specs=in_specs, out_specs=out_specs, check_vma=False
    )
```

profile of v0, /device:TPU:0, one launch (start us, length us, event | category | flops | bytes accessed | tf_op | source)
XLA Modules:
  0.0 1478.2 jit_solution(13351820157895669522)
XLA Ops:
  11.7 2.5 fusion.10
  18.2 2.6 copy.49
  20.8 1.9 fusion.30
  22.8 17.7 %all-gather.18.cloned.1.call-done = bf16[2048,512]{1,0:T(8,128)(2,1)} async-done(((bf16[256,512]{1,0:T(8,128)(2,1)}), bf16[2048,512]{1,0:T(8,128)(2,1)}) %all-gather.18.cloned.1.call-update) | async-done | bytes 2097168 | tf_op jit(solution)/shard_map/all_gather | solution.py:133
  40.4 82.9 %all-gather.12.cloned.1.call-done = bf16[1024,2048]{1,0:T(8,128)(2,1)} async-done(((bf16[256,2048]{1,0:T(8,128)(2,1)}), bf16[1024,2048]{1,0:T(8,128)(2,1)}) %all-gather.12.cloned.1.call-update) | async-done | bytes 4194320 | tf_op jit(solution)/shard_map/all_gather | solution.py:144
  123.3 5.2 fusion.41
  132.0 3.2 copy.78
  135.2 16.4 %all-gather.16.cloned.1.call-done = bf16[2048,512]{1,0:T(8,128)(2,1)} async-done(((bf16[256,512]{1,0:T(8,128)(2,1)}), bf16[2048,512]{1,0:T(8,128)(2,1)}) %all-gather.16.cloned.1.call-update) | async-done | bytes 2097168 | tf_op jit(solution)/shard_map/all_gather | solution.py:132
  151.5 5.2 fusion.40
  158.3 3.2 copy.77
  161.5 3.2 copy.76
  164.6 4.0 fusion.25
  170.7 8.5 fusion.39
  179.2 1.9 all-gather.14.cloned.1.call-done
  181.1 5.2 convolution_convert_fusion.9
  186.3 8.6 fusion
  195.6 7.6 fusion.21
  203.2 7.8 all-gather.20.cloned.1.call-done
  210.9 7.2 fusion.42
  219.0 144.0 %reduce-scatter.12.cloned.1.call-done = f32[256,2048]{1,0:T(8,128)} async-done(((f32[1024,2048]{1,0:T(8,128)}), f32[256,2048]{1,0:T(8,128)}) %reduce-scatter.12.cloned.1.call-update) | async-done | bytes 2097168 | tf_op jit(solution)/shard_map/reduce_scatter | solution.py:159
  363.0 1.9 fusion.36
  368.6 51.1 %all-gather.26.cloned.1.call-done = bf16[2048,2048]{1,0:T(8,128)(2,1)} async-done(((bf16[256,2048]{1,0:T(8,128)(2,1)}), bf16[2048,2048]{1,0:T(8,128)(2,1)}) %all-gather.26.cloned.1.call-update) | async-done | bytes 8388624 | tf_op jit(solution)/shard_map/all_gather | solution.py:137
  419.7 82.9 %all-gather.22.cloned.1.call-done = bf16[1024,2048]{1,0:T(8,128)(2,1)} async-done(((bf16[256,2048]{1,0:T(8,128)(2,1)}), bf16[1024,2048]{1,0:T(8,128)(2,1)}) %all-gather.22.cloned.1.call-update) | async-done | bytes 4194320 | tf_op jit(solution)/shard_map/all_gather | solution.py:164
  502.6 14.7 fusion.44
  517.3 40.0 %all-gather.24.cloned.1.call-done = bf16[2048,2048]{1,0:T(8,128)(2,1)} async-done(((bf16[256,2048]{1,0:T(8,128)(2,1)}), bf16[2048,2048]{1,0:T(8,128)(2,1)}) %all-gather.24.cloned.1.call-update) | async-done | bytes 8388624 | tf_op jit(solution)/shard_map/all_gather | solution.py:136
  557.3 14.5 fusion.43
  571.8 67.7 %all-gather.30.cloned.1.call-done = bf16[1024,2048]{1,0:T(8,128)(2,1)} async-done(((bf16[256,2048]{1,0:T(8,128)(2,1)}), bf16[1024,2048]{1,0:T(8,128)(2,1)}) %all-gather.30.cloned.1.call-update) | async-done | bytes 4194320 | tf_op jit(solution)/shard_map/all_gather | solution.py:174
  639.5 56.3 %all-gather.28.cloned.1.call-done = bf16[2048,2048]{1,0:T(8,128)(2,1)} async-done(((bf16[2048,256]{1,0:T(8,128)(2,1)}), bf16[2048,2048]{1,0:T(8,128)(2,1)}) %all-gather.28.cloned.1.call-update) | async-done | bytes 8388624 | tf_op jit(solution)/shard_map/all_gather | solution.py:138
  695.8 21.8 %multiply_convert_fusion.1 = (bf16[1024,2048]{1,0:T(8,128)(2,1)}, bf16[1024,2048]{1,0:T(8,128)(2,1)}, bf16[1024,2048]{1,0:T(8,128)(2,1)}) fusion(f32[1024,2048]{1,0:T(8,128)} %fusion.43, f32[1024,2048]{1,0:T(8,128)} %fusion.44, bf16[1024,2048]{1,0:T(8,128)(2,1)} %all-gather.30.cloned.1.call-done, bf16[2048,2048]{1,0:T(8,128)(2,1)} %all-gather.28.cloned.1.call-done), kind=kOutput, calls=%fused_computation.12 | convolution fusion | flops 8623489024 | bytes 41943040 | tf_op jit(solution)/shard_map/dot_general | solution.py:25
  717.6 13.1 fusion.45
  730.8 12.9 add_convert_fusion.1
  743.8 13.9 convolution_convert_fusion.3
  757.9 62.7 %reduce-scatter.16.cloned.1.call-done = bf16[256,2048]{1,0:T(8,128)(2,1)} async-done(((bf16[1024,2048]{1,0:T(8,128)(2,1)}), bf16[256,2048]{1,0:T(8,128)(2,1)}) %reduce-scatter.16.cloned.1.call-update) | async-done | bytes 1048592 | tf_op jit(solution)/shard_map/reduce_scatter | solution.py:181
  822.5 77.8 %reduce-scatter.14.cloned.1.call-done = bf16[256,2048]{1,0:T(8,128)(2,1)} async-done(((bf16[1024,2048]{1,0:T(8,128)(2,1)}), bf16[256,2048]{1,0:T(8,128)(2,1)}) %reduce-scatter.14.cloned.1.call-update) | async-done | bytes 1048592 | tf_op jit(solution)/shard_map/reduce_scatter | solution.py:168
  900.3 4.6 fusion.34
  905.0 14.1 convolution_convert_fusion.1
  919.1 14.1 convolution_convert_fusion.2
  933.5 14.1 convolution_convert_fusion
  948.3 38.0 %all-gather.32.cloned.1.call-done = bf16[1024,2048]{1,0:T(8,128)(2,1)} async-done(((bf16[256,2048]{1,0:T(8,128)(2,1)}), bf16[1024,2048]{1,0:T(8,128)(2,1)}) %all-gather.32.cloned.1.call-update) | async-done | bytes 4194320 | tf_op jit(solution)/shard_map/all_gather | solution.py:190
  986.3 5.9 convolution_convert_fusion.4
  992.7 5.9 convolution_convert_fusion.8
  998.6 10.9 fusion.22
  1010.5 3.8 convolution_convert_fusion.5
  1014.3 11.0 multiply_reduce_fusion
  1025.5 12.6 multiply_convert_fusion
  1038.1 3.4 multiply_bitcast_fusion.1
  1041.6 2.4 multiply_bitcast_fusion
  1047.4 6.3 convolution_convert_fusion.7
  1055.1 6.4 convolution_convert_fusion.6
  1061.6 4.5 fusion.47
  1066.1 2.4 fusion.46
  1068.5 6.4 add_convert_fusion
  1074.9 2.9 convert_element_type.182
  1077.8 56.7 %reduce-scatter.28.cloned.1.call-done = bf16[256,2048]{1,0:T(8,128)(2,1)} async-done(((bf16[2048,2048]{1,0:T(8,128)(2,1)}), bf16[256,2048]{1,0:T(8,128)(2,1)}) %reduce-scatter.28.cloned.1.call-update) | async-done | bytes 1048592 | tf_op jit(solution)/shard_map/reduce_scatter | solution.py:229
  1134.5 2.8 convert_element_type.180
  1137.3 71.8 %reduce-scatter.32.cloned.1.call-done = bf16[2048,256]{1,0:T(8,128)(2,1)} async-done(((bf16[2048,2048]{1,0:T(8,128)(2,1)}), bf16[2048,256]{1,0:T(8,128)(2,1)}) %reduce-scatter.32.cloned.1.call-update) | async-done | bytes 1048592 | tf_op jit(solution)/shard_map/reduce_scatter | solution.py:235
  1209.1 2.7 convert_element_type.184
  1211.8 41.6 %reduce-scatter.26.cloned.1.call-done = bf16[512,256]{1,0:T(8,128)(2,1)} async-done(((bf16[512,2048]{1,0:T(8,128)(2,1)}), bf16[512,256]{1,0:T(8,128)(2,1)}) %reduce-scatter.26.cloned.1.call-update) | async-done | bytes 262160 | tf_op jit(solution)/shard_map/reduce_scatter | solution.py:226
  1255.2 42.6 %reduce-scatter.24.cloned.1.call-done = bf16[256,512]{1,0:T(8,128)(2,1)} async-done(((bf16[2048,512]{1,0:T(8,128)(2,1)}), bf16[256,512]{1,0:T(8,128)(2,1)}) %reduce-scatter.24.cloned.1.call-update) | async-done | bytes 262160 | tf_op jit(solution)/shard_map/reduce_scatter | solution.py:223
  1299.7 42.5 %reduce-scatter.20.cloned.1.call-done = bf16[256,512]{1,0:T(8,128)(2,1)} async-done(((bf16[2048,512]{1,0:T(8,128)(2,1)}), bf16[256,512]{1,0:T(8,128)(2,1)}) %reduce-scatter.20.cloned.1.call-update) | async-done | bytes 262160 | tf_op jit(solution)/shard_map/reduce_scatter | solution.py:217
  1343.9 42.6 %reduce-scatter.22.cloned.1.call-done = bf16[256,512]{1,0:T(8,128)(2,1)} async-done(((bf16[2048,512]{1,0:T(8,128)(2,1)}), bf16[256,512]{1,0:T(8,128)(2,1)}) %reduce-scatter.22.cloned.1.call-update) | async-done | bytes 262160 | tf_op jit(solution)/shard_map/reduce_scatter | solution.py:220
  1388.4 77.3 %reduce-scatter.18.cloned.1.call-done = bf16[256,2048]{1,0:T(8,128)(2,1)} async-done(((bf16[1024,2048]{1,0:T(8,128)(2,1)}), bf16[256,2048]{1,0:T(8,128)(2,1)}) %reduce-scatter.18.cloned.1.call-update) | async-done | bytes 1048592 | tf_op jit(solution)/shard_map/reduce_scatter | solution.py:198
  1465.7 1.9 convert_reduce_fusion
  1467.6 3.3 fusion.13
  (149 shorter events, 37.4 us)
Async XLA Ops:
  7.2 9.0 copy-start.31
  7.2 33.2 %all-gather.18.cloned.1.call-start = ((), (), s32[]{:S(2)}) async-start(), calls=%async_computation.14 | async-start | bytes 2359296 | tf_op jit(solution)/shard_map/all_gather | solution.py:133
  7.9 115.4 %all-gather.12.cloned.1.call-start = ((), (), s32[]{:S(2)}) async-start(), calls=%async_computation.11 | async-start | bytes 5242880 | tf_op jit(solution)/shard_map/all_gather | solution.py:144
  9.4 1.7 copy-start.27
  11.1 0.6 copy-start.29
  14.2 137.3 %all-gather.16.cloned.1.call-start = ((), (), s32[]{:S(2)}) async-start(), calls=%async_computation.13 | async-start | bytes 2359296 | tf_op jit(solution)/shard_map/all_gather | solution.py:132
  15.0 166.1 %all-gather.14.cloned.1.call-start = ((), (), s32[]{:S(2)}) async-start(), calls=%async_computation.12 | async-start | bytes 2359296 | tf_op jit(solution)/shard_map/all_gather | solution.py:134
  15.5 195.4 %all-gather.20.cloned.1.call-start = ((), (), s32[]{:S(2)}) async-start(), calls=%async_computation.15 | async-start | bytes 2359296 | tf_op jit(solution)/shard_map/all_gather | solution.py:135
  16.1 346.8 %reduce-scatter.12.cloned.1.call-start = ((), (), s32[]{:S(2)}) async-start(), calls=%async_computation.16 | async-start | bytes 10485760 | tf_op jit(solution)/shard_map/reduce_scatter | solution.py:159
  22.7 141.9 %copy-start.3 = (f32[1024,64]{1,0:T(8,128)}, f32[1024,64]{1,0:T(8,128)S(1)}, u32[]{:S(2)}) copy-start(f32[1024,64]{1,0:T(8,128)S(1)} %get-tuple-element.88) | copy-start | bytes 786436
  22.7 141.9 %copy-start.5 = (f32[1024,64]{1,0:T(8,128)}, f32[1024,64]{1,0:T(8,128)S(1)}, u32[]{:S(2)}) copy-start(f32[1024,64]{1,0:T(8,128)S(1)} %get-tuple-element.89) | copy-start | bytes 786436
  164.6 6.0 copy-start.16
  168.7 1.0 copy-start.8
  168.7 1.3 copy-start.10
  168.7 1.6 copy-start.19
  168.7 2.0 copy-start.21
  179.2 15.8 %copy-start.23 = (f32[4,1024]{1,0:T(4,128)}, f32[4,1024]{1,0:T(4,128)S(1)}, u32[]{:S(2)}) copy-start(f32[4,1024]{1,0:T(4,128)S(1)} %get-tuple-element.90) | copy-start | bytes 49156
  186.3 8.7 copy-start.14
  195.0 0.6 copy-start.25
  203.2 15.0 %copy-start.34 = (bf16[4,128,1024]{2,1,0:T(8,128)(2,1)}, bf16[4,128,1024]{2,1,0:T(8,128)(2,1)S(1)}, u32[]{:S(2)}) copy-start(bf16[4,128,1024]{2,1,0:T(8,128)(2,1)S(1)} %fusion.21) | copy-start | bytes 3145732
  218.2 144.8 %copy-start = (bf16[256,2048]{1,0:T(8,128)(2,1)S(1)}, bf16[256,2048]{1,0:T(8,128)(2,1)}, u32[]{:S(2)}) copy-start(bf16[256,2048]{1,0:T(8,128)(2,1)} %param.10) | copy-start | bytes 3145732
  218.2 201.6 %all-gather.26.cloned.1.call-start = ((), (), s32[]{:S(2)}) async-start(), calls=%async_computation.19 | async-start | bytes 9437184 | tf_op jit(solution)/shard_map/all_gather | solution.py:137
  218.9 283.7 %all-gather.22.cloned.1.call-start = ((), (), s32[]{:S(2)}) async-start(), calls=%async_computation.17 | async-start | bytes 5242880 | tf_op jit(solution)/shard_map/all_gather | solution.py:164
  366.5 190.8 %all-gather.24.cloned.1.call-start = ((), (), s32[]{:S(2)}) async-start(), calls=%async_computation.18 | async-start | bytes 9437184 | tf_op jit(solution)/shard_map/all_gather | solution.py:136
  367.2 272.3 %all-gather.30.cloned.1.call-start = ((), (), s32[]{:S(2)}) async-start(), calls=%async_computation.22 | async-start | bytes 5242880 | tf_op jit(solution)/shard_map/all_gather | solution.py:174
  367.8 327.9 %all-gather.28.cloned.1.call-start = ((), (), s32[]{:S(2)}) async-start(), calls=%async_computation.20 | async-start | bytes 9437184 | tf_op jit(solution)/shard_map/all_gather | solution.py:138
  368.6 452.1 %reduce-scatter.16.cloned.1.call-start = ((), (), s32[]{:S(2)}) async-start(), calls=%async_computation.23 | async-start | bytes 5242880 | tf_op jit(solution)/shard_map/reduce_scatter | solution.py:181
  717.6 13.2 copy-start.36
  743.7 156.6 %reduce-scatter.14.cloned.1.call-start = ((), (), s32[]{:S(2)}) async-start(), calls=%async_computation.21 | async-start | bytes 5242880 | tf_op jit(solution)/shard_map/reduce_scatter | solution.py:168
  757.7 142.6 %copy-start.7 = (bf16[256,2048]{1,0:T(8,128)(2,1)S(1)}, bf16[256,2048]{1,0:T(8,128)(2,1)}, u32[]{:S(2)}) copy-start(bf16[256,2048]{1,0:T(8,128)(2,1)} %param.19) | copy-start | bytes 3145732
  757.7 228.7 %all-gather.32.cloned.1.call-start = ((), (), s32[]{:S(2)}) async-start(), calls=%async_computation.24 | async-start | bytes 5242880 | tf_op jit(solution)/shard_map/all_gather | solution.py:190
  904.9 170.0 %reduce-scatter.30.cloned.1.call-start = ((), (), s32[]{:S(2)}) async-start(), calls=%async_computation.31 | async-start | bytes 9437184 | tf_op jit(solution)/shard_map/reduce_scatter | solution.py:232
  919.1 215.4 %reduce-scatter.28.cloned.1.call-start = ((), (), s32[]{:S(2)}) async-start(), calls=%async_computation.30 | async-start | bytes 9437184 | tf_op jit(solution)/shard_map/reduce_scatter | solution.py:229
  933.3 275.9 %reduce-scatter.32.cloned.1.call-start = ((), (), s32[]{:S(2)}) async-start(), calls=%async_computation.32 | async-start | bytes 9437184 | tf_op jit(solution)/shard_map/reduce_scatter | solution.py:235
  947.6 0.7 copy-start.24
  947.6 0.7 copy-start.26
  947.6 38.8 %copy-start.35 = (bf16[4,128,1024]{2,1,0:T(8,128)(2,1)S(1)}, bf16[4,128,1024]{2,1,0:T(8,128)(2,1)}, u32[]{:S(2)}) copy-start(bf16[4,128,1024]{2,1,0:T(8,128)(2,1)} %copy-done.34) | copy-start | bytes 3145732
  947.6 305.8 %reduce-scatter.26.cloned.1.call-start = ((), (), s32[]{:S(2)}) async-start(), calls=%async_computation.29 | async-start | bytes 2359296 | tf_op jit(solution)/shard_map/reduce_scatter | solution.py:226
  992.3 305.6 %reduce-scatter.24.cloned.1.call-start = ((), (), s32[]{:S(2)}) async-start(), calls=%async_computation.28 | async-start | bytes 2359296 | tf_op jit(solution)/shard_map/reduce_scatter | solution.py:223
  998.6 11.9 copy-start.32
  1009.5 1.0 copy-start.12
  1010.5 3.8 copy-start.15
  1025.3 316.9 %reduce-scatter.20.cloned.1.call-start = ((), (), s32[]{:S(2)}) async-start(), calls=%async_computation.26 | async-start | bytes 2359296 | tf_op jit(solution)/shard_map/reduce_scatter | solution.py:217
  1025.5 12.6 copy-start.9
  1025.5 12.6 copy-start.11
  1038.1 3.4 copy-start.20
  1038.1 3.4 copy-start.22
  1041.6 2.4 copy-start.4
  1041.6 2.4 copy-start.6
  1053.7 332.9 %reduce-scatter.22.cloned.1.call-start = ((), (), s32[]{:S(2)}) async-start(), calls=%async_computation.27 | async-start | bytes 2359296 | tf_op jit(solution)/shard_map/reduce_scatter | solution.py:220
  1055.1 6.4 copy-start.18
  1061.5 4.5 copy-start.17
  1061.5 404.2 %reduce-scatter.18.cloned.1.call-start = ((), (), s32[]{:S(2)}) async-start(), calls=%async_computation.25 | async-start | bytes 5242880 | tf_op jit(solution)/shard_map/reduce_scatter | solution.py:198
  1061.6 4.5 copy-start.33
  1066.0 2.4 copy-start.13
  1077.8 387.8 %copy-start.1 = (bf16[256,2048]{1,0:T(8,128)(2,1)S(1)}, bf16[256,2048]{1,0:T(8,128)(2,1)}, u32[]{:S(2)}) copy-start(bf16[256,2048]{1,0:T(8,128)(2,1)} %param.10) | copy-start | bytes 3145732
  1077.8 387.8 %copy-start.28 = (f32[256]{0:T(256)S(1)}, f32[256]{0:T(256)}, u32[]{:S(2)}) copy-start(f32[256]{0:T(256)} %copy-done.27) | copy-start | bytes 3076
  1077.8 387.8 %copy-start.30 = (f32[256]{0:T(256)S(1)}, f32[256]{0:T(256)}, u32[]{:S(2)}) copy-start(f32[256]{0:T(256)} %copy-done.29) | copy-start | bytes 3076
  1137.3 330.3 %copy-start.2 = (f32[256,2048]{1,0:T(8,128)S(1)}, f32[256,2048]{1,0:T(8,128)}, u32[]{:S(2)}) copy-start(f32[256,2048]{1,0:T(8,128)} %get-tuple-element.55) | copy-start | bytes 6291460
Sparse Core Ops, SparseCore 0:
  9.9 30.4 all-gather.17
  42.6 80.7 all-gather.11
  125.2 26.2 all-gather.15
  153.3 27.7 all-gather.13
  182.8 28.0 all-gather.19
  218.3 144.6 reduce-scatter.11
  364.8 54.8 all-gather.25
  421.9 80.7 all-gather.21
  504.5 52.7 all-gather.23
  558.7 80.7 all-gather.29
  641.4 54.3 all-gather.27
  743.8 76.7 reduce-scatter.15
  822.9 77.2 reduce-scatter.13
  905.1 81.2 all-gather.31
  989.7 69.9 reduce-scatter.29
  1063.0 71.4 reduce-scatter.27
  1137.8 71.2 reduce-scatter.31
  1212.3 41.1 reduce-scatter.25
  1256.7 41.0 reduce-scatter.23
  1301.0 41.1 reduce-scatter.19
  1345.4 41.0 reduce-scatter.21
  1388.9 76.7 reduce-scatter.17
where the time goes:
time: 1490 us; the launch traced here: 1480 us
  waiting for transfers between devices  1130 us (76%)
  matrix products  241 us (16%)
  other arithmetic  68.2 us (5%)
  local copies, waits for them, and re-layouts  23.8 us (2%)
  between operations  15.3 us (1%)
    reduce_scatter x1, waiting for transfers between devices, per_device(): lax.psum_scatter(product(attended, full_output), 'row', scatter_dimension...  144 us
    all_gather x1, waiting for transfers between devices, per_device(): first_rows = lax.all_gather(normed_first, 'row', axis=0, tiled=True)  82.9 us
    all_gather x1, waiting for transfers between devices, per_device(): second_rows = lax.all_gather(normed_second, 'row', axis=0, tiled=True)  82.9 us
    reduce_scatter x1, waiting for transfers between devices, per_device(): lax.psum_scatter(product(activation, full_down).astype(jnp.bfloat16), 'ro...  77.8 us
    reduce_scatter x1, waiting for transfers between devices, per_device(): lax.psum_scatter((times_transpose(grad_query, back_query) + times_transpo...  77.3 us
    reduce_scatter x1, waiting for transfers between devices, per_device(): lax.psum_scatter(grad_down_w.astype(jnp.bfloat16), 'col', scatter_dimensi...  71.8 us
    all_gather x1, waiting for transfers between devices, per_device(): grad_rows = lax.all_gather(cotangent, 'row', axis=0, tiled=True)  67.7 us
    dot_general x7, matrix products, times_transpose(): lax.dot_general(left, right, (((1,), (1,)), ((), ())), preferred_element_...  67 us
  transfers between devices with their start and end apart: 22, of which 21 were waited for; matrix products, arithmetic and copies ran while one was open for 18% of the time, Pallas kernels for 0%

commit v1 on v0

--- a/solution.py
+++ b/solution.py
@@ -171,7 +171,16 @@
     output = (middle + ffn_sum).astype(jnp.bfloat16)
     back_query, back_key, back_value, back_output = (full_query, full_key, full_value, full_output)
     back_gate, back_up, back_down = (full_gate, full_up, full_down)
-    grad_rows = lax.all_gather(cotangent, "row", axis=0, tiled=True)
+    ways = lax.axis_size("row")
+    up = [(d, (d + 1) % ways) for d in range(ways)]
+    down = [(d, (d - 1) % ways) for d in range(ways)]
+    earlier, later = ([cotangent], [cotangent])
+    for _ in range(ways // 2):
+        earlier.append(lax.ppermute(earlier[-1], "row", up))
+    for _ in range((ways - 1) // 2):
+        later.append(lax.ppermute(later[-1], "row", down))
+    line = jnp.concatenate([*earlier[::-1], *later[1:]], axis=0)
+    grad_rows = jnp.roll(line, (lax.axis_index("row") - ways // 2) * cotangent.shape[0], axis=0)
     grad_activation = times_transpose(grad_rows, back_down)
     sigma = jax.nn.sigmoid(gate_lin)
     grad_gate = (grad_activation * up_lin * sigma * (1.0 + gate_lin * (1.0 - sigma))).astype(

time: 1490 us -> 1420 us (0.953)
  waiting for transfers between devices: 1130 us -> 1030 us
  local copies, waits for them, and re-layouts: 23.8 us -> 39.8 us
    ppermute x0 -> x3, waiting for transfers between devices: none -> 80.9 us  [the longest x2 49.5 us: per_device(): earlier.append(lax.ppermute(earlier[-1], 'row', up))]
    reduce_scatter x1, waiting for transfers between devices: 71.8 us -> 0.02 us  [per_device(): lax.psum_scatter(grad_down_w.astype(jnp.bfloat16), 'col', scatter_dimensi...]
    all_gather x1 -> x0, waiting for transfers between devices: 67.7 us -> none  [per_device(): grad_rows = lax.all_gather(cotangent, 'row', axis=0, tiled=True)]
    reduce_scatter x1, waiting for transfers between devices: 0.02 us -> 56.4 us  [per_device(): lax.psum_scatter(grad_up_w.astype(jnp.bfloat16), 'col', scatter_dimension...]
    all_gather x1, waiting for transfers between devices: 51.1 us -> 0.01 us  [per_device(): lax.all_gather(w_up, 'col', axis=0, tiled=True)]
    all_gather x1, waiting for transfers between devices: 82.9 us -> 40.4 us  [per_device(): second_rows = lax.all_gather(normed_second, 'row', axis=0, tiled=True)]
    reduce_scatter x1, waiting for transfers between devices: 56.7 us -> 72.1 us  [per_device(): lax.psum_scatter(grad_gate_w.astype(jnp.bfloat16), 'col', scatter_dimensi...]
    unnamed x78 -> x85, local copies, waits for them, and re-layouts: 16.2 us -> 30 us
  transfers between devices with their start and end apart: 22 -> 24, of which waited for: 21 -> 22; matrix products, arithmetic and copies ran while one was open for 18% -> 20% of each run, Pallas kernels for 0% -> 0%
where the time goes in v1:
time: 1420 us; the launch traced here: 1410 us
  waiting for transfers between devices  1030 us (73%)
  matrix products  241 us (17%)
  other arithmetic  68.3 us (5%)
  local copies, waits for them, and re-layouts  39.8 us (3%)
  between operations  15.3 us (1%)
    reduce_scatter x1, waiting for transfers between devices, per_device(): lax.psum_scatter(product(attended, full_output), 'row', scatter_dimension...  144 us
    all_gather x1, waiting for transfers between devices, per_device(): first_rows = lax.all_gather(normed_first, 'row', axis=0, tiled=True)  82.9 us
    reduce_scatter x1, waiting for transfers between devices, per_device(): lax.psum_scatter(product(activation, full_down).astype(jnp.bfloat16), 'ro...  77.6 us
    reduce_scatter x1, waiting for transfers between devices, per_device(): lax.psum_scatter((times_transpose(grad_query, back_query) + times_transpo...  77.3 us
    reduce_scatter x1, waiting for transfers between devices, per_device(): lax.psum_scatter(grad_gate_w.astype(jnp.bfloat16), 'col', scatter_dimensi...  72.1 us
    dot_general x7, matrix products, times_transpose(): lax.dot_general(left, right, (((1,), (1,)), ((), ())), preferred_element_...  67.1 us
    dot_general x7, matrix products, product(): return jnp.dot(left, right, preferred_element_type=jnp.float32)  65.7 us
    dot_general x7, matrix products, contract_rows(): lax.dot_general(left, right, (((0,), (0,)), ((), ())), preferred_element_...  64.7 us
  transfers between devices with their start and end apart: 24, of which 22 were waited for; matrix products, arithmetic and copies ran while one was open for 20% of the time, Pallas kernels for 0%

profile of v1, /device:TPU:0, one launch (start us, length us, event | category | flops | bytes accessed | tf_op | source)
XLA Modules:
  0.0 1405.1 jit_solution(4308192044159121640)
XLA Ops:
  11.7 2.5 fusion.13
  18.2 2.6 copy.49
  22.7 17.7 %all-gather.17.cloned.1.call-done = bf16[2048,512]{1,0:T(8,128)(2,1)} async-done(((bf16[256,512]{1,0:T(8,128)(2,1)}), bf16[2048,512]{1,0:T(8,128)(2,1)}) %all-gather.17.cloned.1.call-update) | async-done | bytes 2097168 | tf_op jit(solution)/shard_map/all_gather | solution.py:133
  40.4 82.9 %all-gather.11.cloned.1.call-done = bf16[1024,2048]{1,0:T(8,128)(2,1)} async-done(((bf16[256,2048]{1,0:T(8,128)(2,1)}), bf16[1024,2048]{1,0:T(8,128)(2,1)}) %all-gather.11.cloned.1.call-update) | async-done | bytes 4194320 | tf_op jit(solution)/shard_map/all_gather | solution.py:144
  123.3 5.2 fusion.46
  132.0 3.2 copy.78
  135.2 16.4 %all-gather.15.cloned.1.call-done = bf16[2048,512]{1,0:T(8,128)(2,1)} async-done(((bf16[256,512]{1,0:T(8,128)(2,1)}), bf16[2048,512]{1,0:T(8,128)(2,1)}) %all-gather.15.cloned.1.call-update) | async-done | bytes 2097168 | tf_op jit(solution)/shard_map/all_gather | solution.py:132
  151.5 5.2 fusion.45
  158.3 3.2 copy.77
  161.5 3.2 copy.76
  164.6 4.0 fusion.28
  170.7 8.5 fusion.44
  181.1 5.2 convolution_convert_fusion.9
  186.3 8.6 fusion
  195.6 7.6 fusion.24
  203.2 7.8 all-gather.19.cloned.1.call-done
  210.9 7.2 fusion.47
  219.0 144.0 %reduce-scatter.12.cloned.1.call-done = f32[256,2048]{1,0:T(8,128)} async-done(((f32[1024,2048]{1,0:T(8,128)}), f32[256,2048]{1,0:T(8,128)}) %reduce-scatter.12.cloned.1.call-update) | async-done | bytes 2097168 | tf_op jit(solution)/shard_map/reduce_scatter | solution.py:159
  369.0 25.3 %collective-permute-done = bf16[256,2048]{1,0:T(8,128)(2,1)} collective-permute-done((bf16[256,2048]{1,0:T(8,128)(2,1)S(1)}, bf16[256,2048]{1,0:T(8,128)(2,1)}, u32[]{:S(2)}, u32[]{:S(2)}) %collective-permute-start) | collective-permute-done | bytes 1048608 | tf_op jit(solution)/shard_map/ppermute | solution.py:179
  394.4 4.0 collective-permute-start.2
  398.4 24.1 %collective-permute-done.1 = bf16[256,2048]{1,0:T(8,128)(2,1)} collective-permute-done((bf16[256,2048]{1,0:T(8,128)(2,1)}, bf16[256,2048]{1,0:T(8,128)(2,1)}, u32[]{:S(2)}, u32[]{:S(2)}) %collective-permute-start.1) | collective-permute-done | bytes 1048608 | tf_op jit(solution)/shard_map/ppermute | solution.py:179
  428.2 31.4 %collective-permute-done.2 = bf16[256,2048]{1,0:T(8,128)(2,1)} collective-permute-done((bf16[256,2048]{1,0:T(8,128)(2,1)S(1)}, bf16[256,2048]{1,0:T(8,128)(2,1)}, u32[]{:S(2)}, u32[]{:S(2)}) %collective-permute-start.2) | collective-permute-done | bytes 1048608 | tf_op jit(solution)/shard_map/ppermute | solution.py:181
  459.6 2.3 constant_dynamic-update-slice_fusion.4
  461.9 2.3 constant_dynamic-update-slice_fusion.3
  470.0 40.4 %all-gather.21.cloned.1.call-done = bf16[1024,2048]{1,0:T(8,128)(2,1)} async-done(((bf16[256,2048]{1,0:T(8,128)(2,1)}), bf16[1024,2048]{1,0:T(8,128)(2,1)}) %all-gather.21.cloned.1.call-update) | async-done | bytes 4194320 | tf_op jit(solution)/shard_map/all_gather | solution.py:164
  510.4 14.5 %fusion.49 = f32[1024,2048]{1,0:T(8,128)} fusion(bf16[1024,2048]{1,0:T(8,128)(2,1)} %all-gather.21.cloned.1.call-done, bf16[2048,2048]{1,0:T(8,128)(2,1)} %all-gather.25.cloned.1.call-done), kind=kOutput, calls=%fused_computation.116 | convolution fusion | flops 8589934592 | bytes 20971520 | tf_op jit(solution)/shard_map/dot_general | solution.py:15
  524.9 40.5 %all-gather.23.cloned.1.call-done = bf16[2048,2048]{1,0:T(8,128)(2,1)} async-done(((bf16[256,2048]{1,0:T(8,128)(2,1)}), bf16[2048,2048]{1,0:T(8,128)(2,1)}) %all-gather.23.cloned.1.call-update) | async-done | bytes 8388624 | tf_op jit(solution)/shard_map/all_gather | solution.py:136
  565.4 14.4 %fusion.48 = f32[1024,2048]{1,0:T(8,128)} fusion(bf16[1024,2048]{1,0:T(8,128)(2,1)} %all-gather.21.cloned.1.call-done, bf16[2048,2048]{1,0:T(8,128)(2,1)} %all-gather.23.cloned.1.call-done), kind=kOutput, calls=%fused_computation.115 | convolution fusion | flops 8589934592 | bytes 20971520 | tf_op jit(solution)/shard_map/dot_general | solution.py:15
  579.8 43.2 %all-gather.27.cloned.1.call-done = bf16[2048,2048]{1,0:T(8,128)(2,1)} async-done(((bf16[2048,256]{1,0:T(8,128)(2,1)}), bf16[2048,2048]{1,0:T(8,128)(2,1)}) %all-gather.27.cloned.1.call-update) | async-done | bytes 8388624 | tf_op jit(solution)/shard_map/all_gather | solution.py:138
  623.0 21.9 %multiply_convert_fusion.1 = (bf16[1024,2048]{1,0:T(8,128)(2,1)}, bf16[1024,2048]{1,0:T(8,128)(2,1)}, bf16[1024,2048]{1,0:T(8,128)(2,1)}) fusion(f32[1024,2048]{1,0:T(8,128)} %fusion.48, f32[1024,2048]{1,0:T(8,128)} %fusion.49, bf16[2048,2048]{1,0:T(8,128)(2,1)} %all-gather.27.cloned.1.call-done, bf16[2048,2048]{1,0:T(8,128)(2,1)} %constant_dynamic-update-slice_fusion, ...), kind=kOutput, calls=%fused_computation.12 | convolution fusion | flops 8623489024 | bytes 41943044 | tf_op jit(solution)/shard_map/dot_general | solution.py:25
  644.9 13.1 fusion.50
  658.0 12.9 add_convert_fusion.1
  671.0 13.9 convolution_convert_fusion.3
  685.2 62.7 %reduce-scatter.16.cloned.1.call-done = bf16[256,2048]{1,0:T(8,128)(2,1)} async-done(((bf16[1024,2048]{1,0:T(8,128)(2,1)}), bf16[256,2048]{1,0:T(8,128)(2,1)}) %reduce-scatter.16.cloned.1.call-update) | async-done | bytes 1048592 | tf_op jit(solution)/shard_map/reduce_scatter | solution.py:190
  749.8 77.6 %reduce-scatter.14.cloned.1.call-done = bf16[256,2048]{1,0:T(8,128)(2,1)} async-done(((bf16[1024,2048]{1,0:T(8,128)(2,1)}), bf16[256,2048]{1,0:T(8,128)(2,1)}) %reduce-scatter.14.cloned.1.call-update) | async-done | bytes 1048592 | tf_op jit(solution)/shard_map/reduce_scatter | solution.py:168
  827.4 4.6 fusion.39
  832.1 14.1 %convolution_convert_fusion = bf16[2048,2048]{1,0:T(8,128)(2,1)} fusion(bf16[1024,2048]{1,0:T(8,128)(2,1)} %get-tuple-element.70, bf16[2048,2048]{1,0:T(8,128)(2,1)} %constant_dynamic-update-slice_fusion, s32[]{:T(128)S(6)} %select_n.22), kind=kOutput, calls=%fused_computation.18 | convolution fusion | flops 8594128896 | bytes 16777220 | tf_op jit(solution)/shard_map/dot_general | solution.py:19
  846.2 14.1 %convolution_convert_fusion.1 = bf16[2048,2048]{1,0:T(8,128)(2,1)} fusion(bf16[1024,2048]{1,0:T(8,128)(2,1)} %all-gather.21.cloned.1.call-done, bf16[1024,2048]{1,0:T(8,128)(2,1)} %get-tuple-element.68), kind=kOutput, calls=%fused_computation.19 | convolution fusion | flops 8594128896 | bytes 16777216 | tf_op jit(solution)/shard_map/dot_general | solution.py:19
  860.6 14.1 %convolution_convert_fusion.2 = bf16[2048,2048]{1,0:T(8,128)(2,1)} fusion(bf16[1024,2048]{1,0:T(8,128)(2,1)} %all-gather.21.cloned.1.call-done, bf16[1024,2048]{1,0:T(8,128)(2,1)} %get-tuple-element.69), kind=kOutput, calls=%fused_computation.20 | convolution fusion | flops 8594128896 | bytes 16777216 | tf_op jit(solution)/shard_map/dot_general | solution.py:19
  875.5 38.0 %all-gather.29.cloned.1.call-done = bf16[1024,2048]{1,0:T(8,128)(2,1)} async-done(((bf16[256,2048]{1,0:T(8,128)(2,1)}), bf16[1024,2048]{1,0:T(8,128)(2,1)}) %all-gather.29.cloned.1.call-update) | async-done | bytes 4194320 | tf_op jit(solution)/shard_map/all_gather | solution.py:199
  913.5 5.9 convolution_convert_fusion.4
  919.8 6.1 convolution_convert_fusion.8
  925.9 10.8 fusion.25
  937.7 3.9 convolution_convert_fusion.5
  941.5 11.0 multiply_reduce_fusion
  952.8 12.6 multiply_convert_fusion
  965.4 3.4 multiply_bitcast_fusion.1
  968.9 2.4 multiply_bitcast_fusion
  974.6 6.3 convolution_convert_fusion.7
  982.3 6.4 convolution_convert_fusion.6
  988.8 4.5 fusion.52
  993.3 2.4 fusion.51
  995.7 6.3 add_convert_fusion
  1002.1 2.9 convert_element_type.184
  1005.0 56.4 %reduce-scatter.30.cloned.1.call-done = bf16[256,2048]{1,0:T(8,128)(2,1)} async-done(((bf16[2048,2048]{1,0:T(8,128)(2,1)}), bf16[256,2048]{1,0:T(8,128)(2,1)}) %reduce-scatter.30.cloned.1.call-update) | async-done | bytes 1048592 | tf_op jit(solution)/shard_map/reduce_scatter | solution.py:241
  1061.4 2.8 convert_element_type.182
  1064.2 72.1 %reduce-scatter.28.cloned.1.call-done = bf16[256,2048]{1,0:T(8,128)(2,1)} async-done(((bf16[2048,2048]{1,0:T(8,128)(2,1)}), bf16[256,2048]{1,0:T(8,128)(2,1)}) %reduce-scatter.28.cloned.1.call-update) | async-done | bytes 1048592 | tf_op jit(solution)/shard_map/reduce_scatter | solution.py:238
  1136.2 2.8 convert_element_type.180
  1139.0 41.5 %reduce-scatter.26.cloned.1.call-done = bf16[512,256]{1,0:T(8,128)(2,1)} async-done(((bf16[512,2048]{1,0:T(8,128)(2,1)}), bf16[512,256]{1,0:T(8,128)(2,1)}) %reduce-scatter.26.cloned.1.call-update) | async-done | bytes 262160 | tf_op jit(solution)/shard_map/reduce_scatter | solution.py:235
  1182.3 42.5 %reduce-scatter.24.cloned.1.call-done = bf16[256,512]{1,0:T(8,128)(2,1)} async-done(((bf16[2048,512]{1,0:T(8,128)(2,1)}), bf16[256,512]{1,0:T(8,128)(2,1)}) %reduce-scatter.24.cloned.1.call-update) | async-done | bytes 262160 | tf_op jit(solution)/shard_map/reduce_scatter | solution.py:232
  1226.6 42.6 %reduce-scatter.20.cloned.1.call-done = bf16[256,512]{1,0:T(8,128)(2,1)} async-done(((bf16[2048,512]{1,0:T(8,128)(2,1)}), bf16[256,512]{1,0:T(8,128)(2,1)}) %reduce-scatter.20.cloned.1.call-update) | async-done | bytes 262160 | tf_op jit(solution)/shard_map/reduce_scatter | solution.py:226
  1271.0 42.5 %reduce-scatter.22.cloned.1.call-done = bf16[256,512]{1,0:T(8,128)(2,1)} async-done(((bf16[2048,512]{1,0:T(8,128)(2,1)}), bf16[256,512]{1,0:T(8,128)(2,1)}) %reduce-scatter.22.cloned.1.call-update) | async-done | bytes 262160 | tf_op jit(solution)/shard_map/reduce_scatter | solution.py:229
  1315.3 77.3 %reduce-scatter.18.cloned.1.call-done = bf16[256,2048]{1,0:T(8,128)(2,1)} async-done(((bf16[1024,2048]{1,0:T(8,128)(2,1)}), bf16[256,2048]{1,0:T(8,128)(2,1)}) %reduce-scatter.18.cloned.1.call-update) | async-done | bytes 1048592 | tf_op jit(solution)/shard_map/reduce_scatter | solution.py:207
  1394.6 3.3 fusion.16
  (160 shorter events, 56.8 us)
Async XLA Ops:
  7.2 9.0 copy-start.31
  7.2 33.2 %all-gather.17.cloned.1.call-start = ((), (), s32[]{:S(2)}) async-start(), calls=%async_computation.14 | async-start | bytes 2359296 | tf_op jit(solution)/shard_map/all_gather | solution.py:133
  7.9 115.4 %all-gather.11.cloned.1.call-start = ((), (), s32[]{:S(2)}) async-start(), calls=%async_computation.11 | async-start | bytes 5242880 | tf_op jit(solution)/shard_map/all_gather | solution.py:144
  9.4 1.7 copy-start.27
  11.1 0.6 copy-start.29
  14.2 137.3 %all-gather.15.cloned.1.call-start = ((), (), s32[]{:S(2)}) async-start(), calls=%async_computation.13 | async-start | bytes 2359296 | tf_op jit(solution)/shard_map/all_gather | solution.py:132
  15.0 166.1 %all-gather.13.cloned.1.call-start = ((), (), s32[]{:S(2)}) async-start(), calls=%async_computation.12 | async-start | bytes 2359296 | tf_op jit(solution)/shard_map/all_gather | solution.py:134
  15.5 195.4 %all-gather.19.cloned.1.call-start = ((), (), s32[]{:S(2)}) async-start(), calls=%async_computation.15 | async-start | bytes 2359296 | tf_op jit(solution)/shard_map/all_gather | solution.py:135
  16.1 346.8 %reduce-scatter.12.cloned.1.call-start = ((), (), s32[]{:S(2)}) async-start(), calls=%async_computation.16 | async-start | bytes 10485760 | tf_op jit(solution)/shard_map/reduce_scatter | solution.py:159
  22.7 141.9 %copy-start.4 = (f32[1024,64]{1,0:T(8,128)}, f32[1024,64]{1,0:T(8,128)S(1)}, u32[]{:S(2)}) copy-start(f32[1024,64]{1,0:T(8,128)S(1)} %get-tuple-element.88) | copy-start | bytes 786436
  22.7 141.9 %copy-start.6 = (f32[1024,64]{1,0:T(8,128)}, f32[1024,64]{1,0:T(8,128)S(1)}, u32[]{:S(2)}) copy-start(f32[1024,64]{1,0:T(8,128)S(1)} %get-tuple-element.89) | copy-start | bytes 786436
  164.6 6.0 copy-start.16
  168.7 1.0 copy-start.8
  168.7 1.3 copy-start.10
  168.7 1.6 copy-start.19
  168.7 2.0 copy-start.21
  179.2 15.8 %copy-start.23 = (f32[4,1024]{1,0:T(4,128)}, f32[4,1024]{1,0:T(4,128)S(1)}, u32[]{:S(2)}) copy-start(f32[4,1024]{1,0:T(4,128)S(1)} %get-tuple-element.90) | copy-start | bytes 49156
  186.3 8.7 copy-start.14
  195.0 0.6 copy-start.25
  203.2 15.0 %copy-start.34 = (bf16[4,128,1024]{2,1,0:T(8,128)(2,1)}, bf16[4,128,1024]{2,1,0:T(8,128)(2,1)S(1)}, u32[]{:S(2)}) copy-start(bf16[4,128,1024]{2,1,0:T(8,128)(2,1)S(1)} %fusion.24) | copy-start | bytes 3145732
  218.2 144.8 %copy-start = (bf16[256,2048]{1,0:T(8,128)(2,1)S(1)}, bf16[256,2048]{1,0:T(8,128)(2,1)}, u32[]{:S(2)}) copy-start(bf16[256,2048]{1,0:T(8,128)(2,1)} %param.10) | copy-start | bytes 3145732
  218.2 251.8 %all-gather.25.cloned.1.call-start = ((), (), s32[]{:S(2)}) async-start(), calls=%async_computation.19 | async-start | bytes 9437184 | tf_op jit(solution)/shard_map/all_gather | solution.py:137
  218.9 291.4 %all-gather.21.cloned.1.call-start = ((), (), s32[]{:S(2)}) async-start(), calls=%async_computation.17 | async-start | bytes 5242880 | tf_op jit(solution)/shard_map/all_gather | solution.py:164
  364.8 3.0 copy-start.2
  366.5 198.9 %all-gather.23.cloned.1.call-start = ((), (), s32[]{:S(2)}) async-start(), calls=%async_computation.18 | async-start | bytes 9437184 | tf_op jit(solution)/shard_map/all_gather | solution.py:136
  367.2 255.8 %all-gather.27.cloned.1.call-start = ((), (), s32[]{:S(2)}) async-start(), calls=%async_computation.20 | async-start | bytes 9437184 | tf_op jit(solution)/shard_map/all_gather | solution.py:138
  367.8 380.1 %reduce-scatter.16.cloned.1.call-start = ((), (), s32[]{:S(2)}) async-start(), calls=%async_computation.22 | async-start | bytes 5242880 | tf_op jit(solution)/shard_map/reduce_scatter | solution.py:190
  367.9 26.5 %collective-permute-start = (bf16[256,2048]{1,0:T(8,128)(2,1)S(1)}, bf16[256,2048]{1,0:T(8,128)(2,1)}, u32[]{:S(2)}, u32[]{:S(2)}) collective-permute-start(bf16[256,2048]{1,0:T(8,128)(2,1)S(1)} %copy-done.2), channel_id=1, source_target_pairs={{0,8},{8,16},{16,24},{24,0},{1,9},{9,17},{17,25},{25,1},{2,10},{10... | collective-permute-start | bytes 3145736 | tf_op jit(solution)/shard_map/ppermute | solution.py:179
  394.3 28.2 %collective-permute-start.1 = (bf16[256,2048]{1,0:T(8,128)(2,1)}, bf16[256,2048]{1,0:T(8,128)(2,1)}, u32[]{:S(2)}, u32[]{:S(2)}) collective-permute-start(bf16[256,2048]{1,0:T(8,128)(2,1)} %collective-permute-done), channel_id=1, source_target_pairs={{0,8},{8,16},{16,24},{24,0},{1,9},{9,17},{17,25},{25,1},{2,10},{10... | collective-permute-start | bytes 3145736 | tf_op jit(solution)/shard_map/ppermute | solution.py:179
  394.4 65.2 %collective-permute-start.2 = (bf16[256,2048]{1,0:T(8,128)(2,1)S(1)}, bf16[256,2048]{1,0:T(8,128)(2,1)}, u32[]{:S(2)}, u32[]{:S(2)}) collective-permute-start(bf16[256,2048]{1,0:T(8,128)(2,1)S(1)} %copy-done.2), channel_id=1, source_target_pairs={{0,24},{8,0},{16,8},{24,16},{1,25},{9,1},{17,9},{25,17},{2,26},{10... | collective-permute-start | bytes 3145736 | tf_op jit(solution)/shard_map/ppermute | solution.py:181
  644.9 13.2 copy-start.36
  671.0 156.4 %reduce-scatter.14.cloned.1.call-start = ((), (), s32[]{:S(2)}) async-start(), calls=%async_computation.21 | async-start | bytes 5242880 | tf_op jit(solution)/shard_map/reduce_scatter | solution.py:168
  684.9 228.5 %all-gather.29.cloned.1.call-start = ((), (), s32[]{:S(2)}) async-start(), calls=%async_computation.23 | async-start | bytes 5242880 | tf_op jit(solution)/shard_map/all_gather | solution.py:199
  832.1 170.0 %reduce-scatter.32.cloned.1.call-start = ((), (), s32[]{:S(2)}) async-start(), calls=%async_computation.31 | async-start | bytes 9437184 | tf_op jit(solution)/shard_map/reduce_scatter | solution.py:244
  846.2 215.2 %reduce-scatter.30.cloned.1.call-start = ((), (), s32[]{:S(2)}) async-start(), calls=%async_computation.30 | async-start | bytes 9437184 | tf_op jit(solution)/shard_map/reduce_scatter | solution.py:241
  860.4 275.9 %reduce-scatter.28.cloned.1.call-start = ((), (), s32[]{:S(2)}) async-start(), calls=%async_computation.29 | async-start | bytes 9437184 | tf_op jit(solution)/shard_map/reduce_scatter | solution.py:238
  874.7 0.7 copy-start.24
  874.7 0.7 copy-start.26
  874.7 38.8 %copy-start.35 = (bf16[4,128,1024]{2,1,0:T(8,128)(2,1)S(1)}, bf16[4,128,1024]{2,1,0:T(8,128)(2,1)}, u32[]{:S(2)}) copy-start(bf16[4,128,1024]{2,1,0:T(8,128)(2,1)} %copy-done.34) | copy-start | bytes 3145732
  874.7 305.8 %reduce-scatter.26.cloned.1.call-start = ((), (), s32[]{:S(2)}) async-start(), calls=%async_computation.28 | async-start | bytes 2359296 | tf_op jit(solution)/shard_map/reduce_scatter | solution.py:235
  919.4 305.4 %reduce-scatter.24.cloned.1.call-start = ((), (), s32[]{:S(2)}) async-start(), calls=%async_computation.27 | async-start | bytes 2359296 | tf_op jit(solution)/shard_map/reduce_scatter | solution.py:232
  925.9 11.8 copy-start.32
  936.7 1.0 copy-start.12
  937.6 3.9 copy-start.15
  952.5 316.7 %reduce-scatter.20.cloned.1.call-start = ((), (), s32[]{:S(2)}) async-start(), calls=%async_computation.25 | async-start | bytes 2359296 | tf_op jit(solution)/shard_map/reduce_scatter | solution.py:226
  952.7 12.6 copy-start.9
  952.8 12.6 copy-start.11
  965.4 3.4 copy-start.20
  965.4 3.4 copy-start.22
  968.8 2.4 copy-start.5
  968.8 2.4 copy-start.7
  980.9 332.6 %reduce-scatter.22.cloned.1.call-start = ((), (), s32[]{:S(2)}) async-start(), calls=%async_computation.26 | async-start | bytes 2359296 | tf_op jit(solution)/shard_map/reduce_scatter | solution.py:229
  982.3 6.4 copy-start.18
  988.8 4.5 copy-start.17
  988.8 403.9 %reduce-scatter.18.cloned.1.call-start = ((), (), s32[]{:S(2)}) async-start(), calls=%async_computation.24 | async-start | bytes 5242880 | tf_op jit(solution)/shard_map/reduce_scatter | solution.py:207
  988.8 4.5 copy-start.33
  993.3 2.4 copy-start.13
  1005.0 387.7 %copy-start.1 = (bf16[256,2048]{1,0:T(8,128)(2,1)S(1)}, bf16[256,2048]{1,0:T(8,128)(2,1)}, u32[]{:S(2)}) copy-start(bf16[256,2048]{1,0:T(8,128)(2,1)} %param.10) | copy-start | bytes 3145732
  1005.0 387.7 %copy-start.28 = (f32[256]{0:T(256)S(1)}, f32[256]{0:T(256)}, u32[]{:S(2)}) copy-start(f32[256]{0:T(256)} %copy-done.27) | copy-start | bytes 3076
  1005.0 387.7 %copy-start.30 = (f32[256]{0:T(256)S(1)}, f32[256]{0:T(256)}, u32[]{:S(2)}) copy-start(f32[256]{0:T(256)} %copy-done.29) | copy-start | bytes 3076
  1064.2 330.4 %copy-start.3 = (f32[256,2048]{1,0:T(8,128)S(1)}, f32[256,2048]{1,0:T(8,128)}, u32[]{:S(2)}) copy-start(f32[256,2048]{1,0:T(8,128)} %get-tuple-element.55) | copy-start | bytes 6291460
Sparse Core Ops, SparseCore 0:
  9.9 30.4 all-gather.16
  42.6 80.7 all-gather.10
  125.2 26.2 all-gather.14
  153.3 27.7 all-gather.12
  182.8 28.0 all-gather.18
  218.3 144.6 reduce-scatter.11
  364.8 54.8 all-gather.24
  421.9 88.4 all-gather.20
  512.3 53.0 all-gather.22
  567.1 55.8 all-gather.26
  671.1 76.7 reduce-scatter.15
  750.1 77.2 reduce-scatter.13
  832.2 81.2 all-gather.28
  916.8 69.7 reduce-scatter.31
  989.9 71.4 reduce-scatter.29
  1064.7 71.4 reduce-scatter.27
  1139.4 41.1 reduce-scatter.25
  1183.7 41.0 reduce-scatter.23
  1228.1 41.1 reduce-scatter.19
  1272.4 41.1 reduce-scatter.21
  1315.8 76.7 reduce-scatter.17
